TPU v7x, 32 devices: a whole 2x2x4 slice. The times are simulated.
32 devices in a mesh: gx: 4 (over z), gy: 4 (over x, core), gz: 2 (over y).
Axes of the slice: x: 2, y: 2, z: 4, core: 2. Of those that a mesh axis runs over, the one named last changes fastest.
Arguments:
- tokens: bfloat16 [64, 128, 3072], P('gx', ('gy', 'gz')), may hold values from -20 to 20
- grads_out: bfloat16 [64, 128, 3072], P('gx', ('gy', 'gz')), may hold values from -6 to 6
- labels: int32 [64, 128, 16], P('gx', ('gy', 'gz')), may hold values from 0 to 2
- ln_gain: float32 [192], replicated, may hold values from 0.1 to 1.9
- qkv_weight: bfloat16 [192, 576], replicated, may hold values from -0.4375 to 0.4375
- proj_weight: bfloat16 [192, 192], replicated, may hold values from -0.4375 to 0.4375
Outputs:
- grad_tokens: bfloat16 [64, 128, 3072], P('gx', ('gy', 'gz'))
- grad_gain: float32 [192], replicated
- grad_qkv: float32 [110592], replicated
- grad_proj: float32 [36864], replicated
Inputs may be any that keep to these rules, and one draw needn't show every extreme that they name: labels are given on the shifted grid.
All inputs are finite; a program needn't handle non-finite values.
Results may differ from a plain program's by a relative error of at most 0.0087.
Values may be sent and summed in bfloat16 or wider, within the bound.
No kernel may reach another device: no remote copies, remote signals or barrier semaphores. Data moves between devices by JAX's collectives and lax.ppermute only.
A program may use at most 64 MiB of HBM per device.

v0:
```python
import jax
import jax.numpy as jnp
from jax import lax
from jax.sharding import PartitionSpec as P

HEADS = 6
C = 192
WIN = 8
SHIFT = 4
NZ = 16


def passed_along(block, axis, distance):
    devices = range(lax.axis_size(axis))
    route = [((i - distance) % len(devices), i) for i in devices]
    return lax.ppermute(block, axis, route)


def to_windows(values):
    extent_a, extent_b, extent_c = (values.shape[0], values.shape[1], values.shape[2])
    trailing = values.shape[3:]
    shaped = values.reshape(
        (extent_a // WIN, WIN, extent_b // WIN, WIN, extent_c // WIN, WIN) + trailing
    )
    axes_order = (0, 2, 4, 1, 3, 5) + tuple(range(6, 6 + len(trailing)))
    return shaped.transpose(axes_order).reshape((-1, WIN**3) + trailing)


def from_windows(values, extent_a, extent_b, extent_c):
    trailing = values.shape[2:]
    shaped = values.reshape(
        (extent_a // WIN, extent_b // WIN, extent_c // WIN, WIN, WIN, WIN) + trailing
    )
    axes_order = (0, 3, 1, 4, 2, 5) + tuple(range(6, 6 + len(trailing)))
    return shaped.transpose(axes_order).reshape((extent_a, extent_b, extent_c) + trailing)


def window_grads(window_tokens, window_grads_out, mask_keys, ln_gain, qkv_weight, proj_weight):
    channels = window_tokens.shape[1]
    head_size = channels // HEADS
    score_scale = head_size ** (-0.5)
    as_float = window_tokens.astype(jnp.float32)
    row_mean = jnp.mean(as_float, axis=1, keepdims=True)
    centred = as_float - row_mean
    inv_std = lax.rsqrt(jnp.mean(centred * centred, axis=1, keepdims=True) + 1e-05)
    x_hat = centred * inv_std
    normed = (x_hat * ln_gain).astype(jnp.bfloat16)
    qkv_rows = jnp.dot(normed, qkv_weight, preferred_element_type=jnp.float32).astype(jnp.bfloat16)
    queries = qkv_rows[:, :channels].reshape(-1, HEADS, head_size)
    keys_all = qkv_rows[:, channels : 2 * channels].reshape(-1, HEADS, head_size)
    values_all = qkv_rows[:, 2 * channels :].reshape(-1, HEADS, head_size)
    scores = (
        jnp.einsum("ihd,jhd->hij", queries, keys_all, preferred_element_type=jnp.float32)
        * score_scale
    )
    allowed = mask_keys[:, None] == mask_keys[None, :]
    weights = jnp.where(allowed[None], jnp.exp(scores), jnp.float32(0.0))
    softmax_probs = weights / jnp.sum(weights, axis=2, keepdims=True)
    probs_bf = softmax_probs.astype(jnp.bfloat16)
    attended = (
        jnp.einsum("hij,jhd->ihd", probs_bf, values_all, preferred_element_type=jnp.float32)
        .reshape(-1, channels)
        .astype(jnp.bfloat16)
    )
    proj_grad = jnp.einsum(
        "tc,td->cd", attended, window_grads_out, preferred_element_type=jnp.float32
    )
    grad_attended = jnp.einsum(
        "tc,dc->td", window_grads_out, proj_weight, preferred_element_type=jnp.float32
    ).astype(jnp.bfloat16)
    grad_heads = grad_attended.reshape(-1, HEADS, head_size)
    grad_probs = jnp.einsum(
        "ihd,jhd->hij", grad_heads, values_all, preferred_element_type=jnp.float32
    )
    grad_values = jnp.einsum(
        "hij,ihd->jhd", probs_bf, grad_heads, preferred_element_type=jnp.float32
    ).astype(jnp.bfloat16)
    row_total = jnp.sum(softmax_probs * grad_probs, axis=2, keepdims=True)
    grad_scores = (softmax_probs * (grad_probs - row_total) * score_scale).astype(jnp.bfloat16)
    grad_queries = jnp.einsum(
        "hij,jhd->ihd", grad_scores, keys_all, preferred_element_type=jnp.float32
    ).astype(jnp.bfloat16)
    grad_keys = jnp.einsum(
        "hij,ihd->jhd", grad_scores, queries, preferred_element_type=jnp.float32
    ).astype(jnp.bfloat16)
    grad_qkv_rows = jnp.concatenate(
        [
            grad_queries.reshape(-1, channels),
            grad_keys.reshape(-1, channels),
            grad_values.reshape(-1, channels),
        ],
        axis=1,
    )
    qkv_grad = jnp.einsum("tc,td->cd", normed, grad_qkv_rows, preferred_element_type=jnp.float32)
    grad_normed = jnp.einsum(
        "td,cd->tc", grad_qkv_rows, qkv_weight, preferred_element_type=jnp.float32
    )
    gain_grad = jnp.sum(grad_normed * x_hat, axis=0)
    scaled_grad = grad_normed * ln_gain
    grad_shifted = inv_std * (
        scaled_grad
        - jnp.mean(scaled_grad, axis=1, keepdims=True)
        - x_hat * jnp.mean(scaled_grad * x_hat, axis=1, keepdims=True)
    )
    return (grad_shifted.astype(jnp.bfloat16), qkv_grad, proj_grad, gain_grad)


def ahead_first(both_arrays):
    arrived = passed_along((both_arrays[0][:SHIFT], both_arrays[1][:SHIFT]), "gx", -1)
    return (
        jnp.concatenate([both_arrays[0][SHIFT:], arrived[0]], axis=0),
        jnp.concatenate([both_arrays[1][SHIFT:], arrived[1]], axis=0),
    )


def ahead_second(both_arrays):
    arrived = passed_along((both_arrays[0][:, :SHIFT], both_arrays[1][:, :SHIFT]), ("gy", "gz"), -1)
    return (
        jnp.concatenate([both_arrays[0][:, SHIFT:], arrived[0]], axis=1),
        jnp.concatenate([both_arrays[1][:, SHIFT:], arrived[1]], axis=1),
    )


def back_first(gradient):
    arrived = passed_along(gradient[-SHIFT:], "gx", 1)
    return jnp.concatenate([arrived, gradient[:-SHIFT]], axis=0)


def back_second(gradient):
    arrived = passed_along(gradient[:, -SHIFT:], ("gy", "gz"), 1)
    return jnp.concatenate([arrived, gradient[:, :-SHIFT]], axis=1)


def per_device(tokens, grads_out, labels, ln_gain, qkv_weight, proj_weight):
    brick_a, brick_b = (tokens.shape[0], tokens.shape[1])
    brick_c = NZ
    channels = C
    both_arrays = (tokens, grads_out)
    both_arrays = ahead_second(ahead_first(both_arrays))
    shifted_tokens = jnp.roll(
        both_arrays[0].reshape(brick_a, brick_b, brick_c, channels), -SHIFT, axis=2
    )
    shifted_grads = jnp.roll(
        both_arrays[1].reshape(brick_a, brick_b, brick_c, channels), -SHIFT, axis=2
    )
    extent_a = brick_a * lax.axis_size("gx")
    extent_b = brick_b * lax.axis_size(("gy", "gz"))
    first_index = lax.axis_index("gx") * brick_a + jnp.arange(brick_a, dtype=jnp.int32)
    second_index = lax.axis_index(("gy", "gz")) * brick_b + jnp.arange(brick_b, dtype=jnp.int32)
    wrap_first = (first_index >= extent_a - SHIFT).astype(jnp.int32)
    wrap_second = (second_index >= extent_b - SHIFT).astype(jnp.int32)
    wrap_third = (jnp.arange(brick_c, dtype=jnp.int32) >= brick_c - SHIFT).astype(jnp.int32)
    region = (
        wrap_first[:, None, None] * 4 + wrap_second[None, :, None] * 2 + wrap_third[None, None, :]
    )
    mask_key = labels * 8 + region

    def window_step(totals, window_item):
        grad_win, qkv_part, proj_part, gain_part = window_grads(
            window_item[0], window_item[1], window_item[2], ln_gain, qkv_weight, proj_weight
        )
        return ((totals[0] + qkv_part, totals[1] + proj_part, totals[2] + gain_part), grad_win)

    zero_sums = (
        jnp.zeros((channels, 3 * channels), jnp.float32),
        jnp.zeros((channels, channels), jnp.float32),
        jnp.zeros((channels,), jnp.float32),
    )
    sums, grad_windows = lax.scan(
        window_step,
        zero_sums,
        (to_windows(shifted_tokens), to_windows(shifted_grads), to_windows(mask_key)),
    )
    qkv_grad, proj_grad, gain_grad = sums
    qkv_grad, proj_grad, gain_grad = lax.psum((qkv_grad, proj_grad, gain_grad), ("gx", "gy", "gz"))
    grad_branch = jnp.roll(from_windows(grad_windows, brick_a, brick_b, brick_c), SHIFT, axis=2)
    grad_branch = grad_branch.reshape(brick_a, brick_b, brick_c * channels)
    grad_branch = back_first(back_second(grad_branch))
    grad_tokens = (grads_out.astype(jnp.float32) + grad_branch.astype(jnp.float32)).astype(
        jnp.bfloat16
    )
    return (grad_tokens, gain_grad, qkv_grad.reshape(-1), proj_grad.reshape(-1))


def solution(mesh):
    return jax.shard_map(
        per_device,
        mesh=mesh,
        in_specs=(
            P("gx", ("gy", "gz"), None),
            P("gx", ("gy", "gz"), None),
            P("gx", ("gy", "gz"), None),
            P(),
            P(),
            P(),
        ),
        out_specs=(P("gx", ("gy", "gz"), None), P(), P(), P()),
        check_vma=False,
    )
```

profile of v0, /device:TPU:0, one launch (start us, length us, event | category | flops | bytes accessed | tf_op | source)
XLA Modules:
  0.0 585.7 jit_solution(5574990165840329090)
XLA Ops:
  9.1 5.0 collective-permute-start.2
  20.2 3.8 collective-permute-done.2
  25.8 5.5 collective-permute-done
  60.5 358.1 %while.17 = (s32[]{:T(128)}, f32[192,576]{1,0:T(8,128)}, f32[192,192]{1,0:T(8,128)S(1)}, f32[192]{0:T(256)S(1)}, bf16[8,512,192]{1,2,0:T(8,128)(2,1)}, /*index=5...) while((s32[]{:T(128)}, f32[192,576]{1,0:T(8,128)}, ...), condition=%wide.region_8.9_spmd.clone, body=%wide.region_0.8_spmd.clone.sunk | while | flops 1079349888 | bytes 64495856 | solution.py:169
  61.6 4.3 fusion.136
  70.8 10.9 %fusion.140 = bf16[6,32,512]{2,1,0:T(8,128)(2,1)} fusion(bf16[512,6,32]{0,2,1:T(8,128)(2,1)S(1)} %bitcast.169, f32[6,512,512]{1,2,0:T(8,128)} %fusion.138, f32[6,512,512]{1,2,0:T(8,128)} %get-tuple-element.265, f32[6,512]{1,0:T(8,128)S(1)} %get-tuple-element.266, pred[512,512]{0,1:T(8,128)(4,1)S(1)} %broadcast_compare_fusion.2), kind=kOutput, calls=%fused_computation.15.clone.1 | convolution fusion | flops 118066688 | bytes 13250560 | tf_op jit(solution)/shard_map/while/body/eval_jaxpr/hij,jhd->ihd/dot_general | solution.py:80
  81.7 10.3 %fusion.139 = bf16[6,32,512]{2,1,0:T(8,128)(2,1)S(1)} fusion(bf16[512,6,32]{0,2,1:T(8,128)(2,1)S(1)} %bitcast.167, f32[6,512,512]{1,2,0:T(8,128)} %fusion.138, f32[6,512,512]{1,2,0:T(8,128)} %get-tuple-element.265, f32[6,512]{1,0:T(8,128)S(1)} %get-tuple-element.266, pred[512,512]{0,1:T(8,128)(4,1)S(1)} %broadcast_compare_fusion.2), kind=kOutput, calls=%fused_computation.16.clone.1 | convolution fusion | flops 118066688 | bytes 13250560 | tf_op jit(solution)/shard_map/while/body/eval_jaxpr/hij,ihd->jhd/dot_general | solution.py:83
  92.0 4.4 fusion.137
  97.7 4.4 fusion.141
  105.4 4.3 fusion.136
  114.6 10.9 %fusion.140 = bf16[6,32,512]{2,1,0:T(8,128)(2,1)} fusion(bf16[512,6,32]{0,2,1:T(8,128)(2,1)S(1)} %bitcast.169, f32[6,512,512]{1,2,0:T(8,128)} %fusion.138, f32[6,512,512]{1,2,0:T(8,128)} %get-tuple-element.265, f32[6,512]{1,0:T(8,128)S(1)} %get-tuple-element.266, pred[512,512]{0,1:T(8,128)(4,1)S(1)} %broadcast_compare_fusion.2), kind=kOutput, calls=%fused_computation.15.clone.1 | convolution fusion | flops 118066688 | bytes 13250560 | tf_op jit(solution)/shard_map/while/body/eval_jaxpr/hij,jhd->ihd/dot_general | solution.py:80
  125.5 10.3 %fusion.139 = bf16[6,32,512]{2,1,0:T(8,128)(2,1)S(1)} fusion(bf16[512,6,32]{0,2,1:T(8,128)(2,1)S(1)} %bitcast.167, f32[6,512,512]{1,2,0:T(8,128)} %fusion.138, f32[6,512,512]{1,2,0:T(8,128)} %get-tuple-element.265, f32[6,512]{1,0:T(8,128)S(1)} %get-tuple-element.266, pred[512,512]{0,1:T(8,128)(4,1)S(1)} %broadcast_compare_fusion.2), kind=kOutput, calls=%fused_computation.16.clone.1 | convolution fusion | flops 118066688 | bytes 13250560 | tf_op jit(solution)/shard_map/while/body/eval_jaxpr/hij,ihd->jhd/dot_general | solution.py:83
  135.8 4.4 fusion.137
  141.6 4.4 fusion.141
  150.3 4.3 fusion.136
  159.5 10.9 %fusion.140 = bf16[6,32,512]{2,1,0:T(8,128)(2,1)} fusion(bf16[512,6,32]{0,2,1:T(8,128)(2,1)S(1)} %bitcast.169, f32[6,512,512]{1,2,0:T(8,128)} %fusion.138, f32[6,512,512]{1,2,0:T(8,128)} %get-tuple-element.265, f32[6,512]{1,0:T(8,128)S(1)} %get-tuple-element.266, pred[512,512]{0,1:T(8,128)(4,1)S(1)} %broadcast_compare_fusion.2), kind=kOutput, calls=%fused_computation.15.clone.1 | convolution fusion | flops 118066688 | bytes 13250560 | tf_op jit(solution)/shard_map/while/body/eval_jaxpr/hij,jhd->ihd/dot_general | solution.py:80
  170.4 10.3 %fusion.139 = bf16[6,32,512]{2,1,0:T(8,128)(2,1)S(1)} fusion(bf16[512,6,32]{0,2,1:T(8,128)(2,1)S(1)} %bitcast.167, f32[6,512,512]{1,2,0:T(8,128)} %fusion.138, f32[6,512,512]{1,2,0:T(8,128)} %get-tuple-element.265, f32[6,512]{1,0:T(8,128)S(1)} %get-tuple-element.266, pred[512,512]{0,1:T(8,128)(4,1)S(1)} %broadcast_compare_fusion.2), kind=kOutput, calls=%fused_computation.16.clone.1 | convolution fusion | flops 118066688 | bytes 13250560 | tf_op jit(solution)/shard_map/while/body/eval_jaxpr/hij,ihd->jhd/dot_general | solution.py:83
  180.7 4.4 fusion.137
  186.4 4.4 fusion.141
  195.2 4.3 fusion.136
  204.3 10.9 %fusion.140 = bf16[6,32,512]{2,1,0:T(8,128)(2,1)} fusion(bf16[512,6,32]{0,2,1:T(8,128)(2,1)S(1)} %bitcast.169, f32[6,512,512]{1,2,0:T(8,128)} %fusion.138, f32[6,512,512]{1,2,0:T(8,128)} %get-tuple-element.265, f32[6,512]{1,0:T(8,128)S(1)} %get-tuple-element.266, pred[512,512]{0,1:T(8,128)(4,1)S(1)} %broadcast_compare_fusion.2), kind=kOutput, calls=%fused_computation.15.clone.1 | convolution fusion | flops 118066688 | bytes 13250560 | tf_op jit(solution)/shard_map/while/body/eval_jaxpr/hij,jhd->ihd/dot_general | solution.py:80
  215.2 10.3 %fusion.139 = bf16[6,32,512]{2,1,0:T(8,128)(2,1)S(1)} fusion(bf16[512,6,32]{0,2,1:T(8,128)(2,1)S(1)} %bitcast.167, f32[6,512,512]{1,2,0:T(8,128)} %fusion.138, f32[6,512,512]{1,2,0:T(8,128)} %get-tuple-element.265, f32[6,512]{1,0:T(8,128)S(1)} %get-tuple-element.266, pred[512,512]{0,1:T(8,128)(4,1)S(1)} %broadcast_compare_fusion.2), kind=kOutput, calls=%fused_computation.16.clone.1 | convolution fusion | flops 118066688 | bytes 13250560 | tf_op jit(solution)/shard_map/while/body/eval_jaxpr/hij,ihd->jhd/dot_general | solution.py:83
  225.5 4.4 fusion.137
  231.3 4.4 fusion.141
  240.0 4.3 fusion.136
  249.2 10.9 %fusion.140 = bf16[6,32,512]{2,1,0:T(8,128)(2,1)} fusion(bf16[512,6,32]{0,2,1:T(8,128)(2,1)S(1)} %bitcast.169, f32[6,512,512]{1,2,0:T(8,128)} %fusion.138, f32[6,512,512]{1,2,0:T(8,128)} %get-tuple-element.265, f32[6,512]{1,0:T(8,128)S(1)} %get-tuple-element.266, pred[512,512]{0,1:T(8,128)(4,1)S(1)} %broadcast_compare_fusion.2), kind=kOutput, calls=%fused_computation.15.clone.1 | convolution fusion | flops 118066688 | bytes 13250560 | tf_op jit(solution)/shard_map/while/body/eval_jaxpr/hij,jhd->ihd/dot_general | solution.py:80
  260.1 10.3 %fusion.139 = bf16[6,32,512]{2,1,0:T(8,128)(2,1)S(1)} fusion(bf16[512,6,32]{0,2,1:T(8,128)(2,1)S(1)} %bitcast.167, f32[6,512,512]{1,2,0:T(8,128)} %fusion.138, f32[6,512,512]{1,2,0:T(8,128)} %get-tuple-element.265, f32[6,512]{1,0:T(8,128)S(1)} %get-tuple-element.266, pred[512,512]{0,1:T(8,128)(4,1)S(1)} %broadcast_compare_fusion.2), kind=kOutput, calls=%fused_computation.16.clone.1 | convolution fusion | flops 118066688 | bytes 13250560 | tf_op jit(solution)/shard_map/while/body/eval_jaxpr/hij,ihd->jhd/dot_general | solution.py:83
  270.4 4.4 fusion.137
  276.1 4.4 fusion.141
  284.9 4.3 fusion.136
  294.0 10.9 %fusion.140 = bf16[6,32,512]{2,1,0:T(8,128)(2,1)} fusion(bf16[512,6,32]{0,2,1:T(8,128)(2,1)S(1)} %bitcast.169, f32[6,512,512]{1,2,0:T(8,128)} %fusion.138, f32[6,512,512]{1,2,0:T(8,128)} %get-tuple-element.265, f32[6,512]{1,0:T(8,128)S(1)} %get-tuple-element.266, pred[512,512]{0,1:T(8,128)(4,1)S(1)} %broadcast_compare_fusion.2), kind=kOutput, calls=%fused_computation.15.clone.1 | convolution fusion | flops 118066688 | bytes 13250560 | tf_op jit(solution)/shard_map/while/body/eval_jaxpr/hij,jhd->ihd/dot_general | solution.py:80
  304.9 10.3 %fusion.139 = bf16[6,32,512]{2,1,0:T(8,128)(2,1)S(1)} fusion(bf16[512,6,32]{0,2,1:T(8,128)(2,1)S(1)} %bitcast.167, f32[6,512,512]{1,2,0:T(8,128)} %fusion.138, f32[6,512,512]{1,2,0:T(8,128)} %get-tuple-element.265, f32[6,512]{1,0:T(8,128)S(1)} %get-tuple-element.266, pred[512,512]{0,1:T(8,128)(4,1)S(1)} %broadcast_compare_fusion.2), kind=kOutput, calls=%fused_computation.16.clone.1 | convolution fusion | flops 118066688 | bytes 13250560 | tf_op jit(solution)/shard_map/while/body/eval_jaxpr/hij,ihd->jhd/dot_general | solution.py:83
  315.3 4.4 fusion.137
  321.0 4.4 fusion.141
  329.7 4.3 fusion.136
  338.9 10.9 %fusion.140 = bf16[6,32,512]{2,1,0:T(8,128)(2,1)} fusion(bf16[512,6,32]{0,2,1:T(8,128)(2,1)S(1)} %bitcast.169, f32[6,512,512]{1,2,0:T(8,128)} %fusion.138, f32[6,512,512]{1,2,0:T(8,128)} %get-tuple-element.265, f32[6,512]{1,0:T(8,128)S(1)} %get-tuple-element.266, pred[512,512]{0,1:T(8,128)(4,1)S(1)} %broadcast_compare_fusion.2), kind=kOutput, calls=%fused_computation.15.clone.1 | convolution fusion | flops 118066688 | bytes 13250560 | tf_op jit(solution)/shard_map/while/body/eval_jaxpr/hij,jhd->ihd/dot_general | solution.py:80
  349.8 10.3 %fusion.139 = bf16[6,32,512]{2,1,0:T(8,128)(2,1)S(1)} fusion(bf16[512,6,32]{0,2,1:T(8,128)(2,1)S(1)} %bitcast.167, f32[6,512,512]{1,2,0:T(8,128)} %fusion.138, f32[6,512,512]{1,2,0:T(8,128)} %get-tuple-element.265, f32[6,512]{1,0:T(8,128)S(1)} %get-tuple-element.266, pred[512,512]{0,1:T(8,128)(4,1)S(1)} %broadcast_compare_fusion.2), kind=kOutput, calls=%fused_computation.16.clone.1 | convolution fusion | flops 118066688 | bytes 13250560 | tf_op jit(solution)/shard_map/while/body/eval_jaxpr/hij,ihd->jhd/dot_general | solution.py:83
  360.1 4.4 fusion.137
  365.9 4.4 fusion.141
  374.6 4.3 fusion.136
  383.8 10.9 %fusion.140 = bf16[6,32,512]{2,1,0:T(8,128)(2,1)} fusion(bf16[512,6,32]{0,2,1:T(8,128)(2,1)S(1)} %bitcast.169, f32[6,512,512]{1,2,0:T(8,128)} %fusion.138, f32[6,512,512]{1,2,0:T(8,128)} %get-tuple-element.265, f32[6,512]{1,0:T(8,128)S(1)} %get-tuple-element.266, pred[512,512]{0,1:T(8,128)(4,1)S(1)} %broadcast_compare_fusion.2), kind=kOutput, calls=%fused_computation.15.clone.1 | convolution fusion | flops 118066688 | bytes 13250560 | tf_op jit(solution)/shard_map/while/body/eval_jaxpr/hij,jhd->ihd/dot_general | solution.py:80
  394.7 10.3 %fusion.139 = bf16[6,32,512]{2,1,0:T(8,128)(2,1)S(1)} fusion(bf16[512,6,32]{0,2,1:T(8,128)(2,1)S(1)} %bitcast.167, f32[6,512,512]{1,2,0:T(8,128)} %fusion.138, f32[6,512,512]{1,2,0:T(8,128)} %get-tuple-element.265, f32[6,512]{1,0:T(8,128)S(1)} %get-tuple-element.266, pred[512,512]{0,1:T(8,128)(4,1)S(1)} %broadcast_compare_fusion.2), kind=kOutput, calls=%fused_computation.16.clone.1 | convolution fusion | flops 118066688 | bytes 13250560 | tf_op jit(solution)/shard_map/while/body/eval_jaxpr/hij,ihd->jhd/dot_general | solution.py:83
  405.0 4.4 fusion.137
  410.7 4.4 fusion.141
  428.4 6.9 %collective-permute-start.4 = (bf16[16,4,3072]{2,1,0:T(4,128)(2,1)S(1)}, bf16[16,4,3072]{2,1,0:T(4,128)(2,1)S(1)}, u32[]{:S(2)}, u32[]{:S(2)}) collective-permute-start(bf16[16,4,3072]{2,1,0:T(4,128)(2,1)S(1)} %slice.101), channel_id=1, source_target_pairs={{7,0},{0,1},{1,2},{2,3},{3,4},{4,5},{5,6},{6,7},{15,8},{8,9},{9,10... | collective-permute-start | bytes 1179656 | tf_op jit(solution)/shard_map/ppermute | solution.py:16
  435.3 5.3 collective-permute-done.4
  445.5 41.9 %psum.21 = f32[192]{0:T(256)} all-reduce(f32[192]{0:T(256)S(1)} %get-tuple-element.65), channel_id=1, replica_groups=mesh['gx'=4,'gy'=4,'gz'=2] {'gx','gy','gz'}, use_global_device_ids=true, to_apply=%region_9.10 | all-reduce | flops 192 | bytes 1536 | tf_op jit(solution)/shard_map/psum | solution.py:175
  490.3 85.1 %all-reduce.3.cloned.1.call-done = (f32[110592]{0:T(1024)}, f32[36864]{0:T(1024)}) async-done(((f32[110592]{0:T(1024)}, f32[36864]{0:T(1024)}), (f32[110592]{0:T(1024)}, f32[36864]{0:T(1024)})) %all-reduce.3.cloned.1.call-update) | async-done | bytes 589840 | tf_op jit(solution)/shard_map/psum | solution.py:175
  (256 shorter events, 142.3 us)
Async XLA Ops:
  7.2 9.3 %copy-start.6 = (bf16[16,16,3072]{2,1,0:T(8,128)(2,1)S(1)}, bf16[16,16,3072]{2,1,0:T(8,128)(2,1)}, u32[]{:S(2)}) copy-start(bf16[16,16,3072]{2,1,0:T(8,128)(2,1)} %param.8) | copy-start | bytes 4718596
  7.2 568.3 %all-reduce.3.cloned.1.call-start = ((), (), s32[]{:S(2)}) async-start(), calls=%async_computation | async-start | bytes 1179648 | tf_op jit(solution)/shard_map/psum | solution.py:175
  9.1 14.9 %collective-permute-start.2 = (bf16[4,16,3072]{2,1,0:T(8,128)(2,1)}, bf16[4,16,3072]{2,1,0:T(8,128)(2,1)}, u32[]{:S(2)}, u32[]{:S(2)}) collective-permute-start(bf16[4,16,3072]{2,1,0:T(8,128)(2,1)} %slice.74), channel_id=1, source_target_pairs={{8,0},{16,8},{24,16},{0,24},{9,1},{17,9},{25,17},{1,25},{10,2},{18... | collective-permute-start | bytes 1179656 | tf_op jit(solution)/shard_map/ppermute | solution.py:16
  15.9 15.3 %collective-permute-start = (bf16[4,16,3072]{2,1,0:T(8,128)(2,1)}, bf16[4,16,3072]{2,1,0:T(8,128)(2,1)}, u32[]{:S(2)}, u32[]{:S(2)}) collective-permute-start(bf16[4,16,3072]{2,1,0:T(8,128)(2,1)} %slice.68), channel_id=1, source_target_pairs={{8,0},{16,8},{24,16},{0,24},{9,1},{17,9},{25,17},{1,25},{10,2},{18... | collective-permute-start | bytes 1179656 | tf_op jit(solution)/shard_map/ppermute | solution.py:16
  16.5 1.1 copy-start.8
  16.5 1.8 slice-start
  18.2 1.3 copy-start.4
  25.4 10.4 %collective-permute-start.3 = (bf16[16,4,3072]{2,0,1:T(8,128)(2,1)S(1)}, bf16[16,4,3072]{2,0,1:T(8,128)(2,1)S(1)}, u32[]{:S(2)}, u32[]{:S(2)}) collective-permute-start(bf16[16,4,3072]{2,0,1:T(8,128)(2,1)S(1)} %pad_maximum_fusion.10), channel_id=1, source_target_pairs={{1,0},{2,1},{3,2},{4,3},{5,4},{6,5},{7,6},{0,7},{9,8},{10,9},{11,1... | collective-permute-start | bytes 1179656 | tf_op jit(solution)/shard_map/ppermute | solution.py:16
  33.4 10.8 %collective-permute-start.1 = (bf16[16,4,3072]{2,0,1:T(8,128)(2,1)}, bf16[16,4,3072]{2,0,1:T(8,128)(2,1)S(1)}, u32[]{:S(2)}, u32[]{:S(2)}) collective-permute-start(bf16[16,4,3072]{2,0,1:T(8,128)(2,1)} %pad_maximum_fusion.11), channel_id=1, source_target_pairs={{1,0},{2,1},{3,2},{4,3},{5,4},{6,5},{7,6},{0,7},{9,8},{10,9},{11,1... | collective-permute-start | bytes 1179656 | tf_op jit(solution)/shard_map/ppermute | solution.py:16
  41.7 2.6 copy-start.3
  50.2 1.6 copy-start
  57.5 3.0 copy-start.2
  57.5 3.0 copy-start.5
  57.5 3.0 copy-start.9
  92.0 4.4 copy-start.10
  96.4 1.3 copy-start.11
  97.7 5.6 copy-start.12
  135.8 4.4 copy-start.10
  140.2 1.3 copy-start.11
  141.6 5.6 copy-start.12
  180.7 4.4 copy-start.10
  185.1 1.3 copy-start.11
  186.4 5.6 copy-start.12
  225.5 4.4 copy-start.10
  229.9 1.3 copy-start.11
  231.3 5.6 copy-start.12
  270.4 4.4 copy-start.10
  274.8 1.3 copy-start.11
  276.1 5.6 copy-start.12
  315.2 4.4 copy-start.10
  319.7 1.3 copy-start.11
  321.0 5.6 copy-start.12
  360.1 4.4 copy-start.10
  364.5 1.3 copy-start.11
  365.9 5.6 copy-start.12
  405.0 4.4 copy-start.10
  409.4 1.3 copy-start.11
  410.7 5.6 copy-start.12
  428.1 59.3 %copy-start.1 = (bf16[16,16,3072]{2,1,0:T(8,128)(2,1)S(1)}, bf16[16,16,3072]{2,1,0:T(8,128)(2,1)}, u32[]{:S(2)}) copy-start(bf16[16,16,3072]{2,1,0:T(8,128)(2,1)} %param.9) | copy-start | bytes 4718596
  428.4 12.2 %collective-permute-start.4 = (bf16[16,4,3072]{2,1,0:T(4,128)(2,1)S(1)}, bf16[16,4,3072]{2,1,0:T(4,128)(2,1)S(1)}, u32[]{:S(2)}, u32[]{:S(2)}) collective-permute-start(bf16[16,4,3072]{2,1,0:T(4,128)(2,1)S(1)} %slice.101), channel_id=1, source_target_pairs={{7,0},{0,1},{1,2},{2,3},{3,4},{4,5},{5,6},{6,7},{15,8},{8,9},{9,10... | collective-permute-start | bytes 1179656 | tf_op jit(solution)/shard_map/ppermute | solution.py:16
  440.6 0.8 copy-start.7
  442.2 45.2 %collective-permute-start.5 = (bf16[4,16,3072]{2,1,0:T(8,128)(2,1)}, bf16[4,16,3072]{2,1,0:T(8,128)(2,1)}, u32[]{:S(2)}, u32[]{:S(2)}) collective-permute-start(bf16[4,16,3072]{2,1,0:T(8,128)(2,1)} %pad_maximum_fusion.9), channel_id=1, source_target_pairs={{24,0},{0,8},{8,16},{16,24},{25,1},{1,9},{9,17},{17,25},{26,2},{2,... | collective-permute-start | bytes 1179656 | tf_op jit(solution)/shard_map/ppermute | solution.py:16
Sparse Core Ops, SparseCore 0:
  445.6 129.8 all-reduce.2
where the time goes:
time: 587 us; the launch traced here: 586 us
  matrix products  347 us (59%)
  waiting for transfers between devices  99.7 us (17%)
  local copies, waits for them, and re-layouts  46.5 us (8%)
  blocking collectives  41.9 us (7%)
  other arithmetic  21.2 us (4%)
  between operations  14.3 us (2%)
  starting transfers between devices  14 us (2%)
    dot_general x8, matrix products, window_grads(): jnp.einsum('hij,jhd->ihd', grad_scores, keys_all, preferred_element_type=...  87.2 us
    psum x1, waiting for transfers between devices, per_device(): lax.psum((qkv_grad, proj_grad, gain_grad), ('gx', 'gy', 'gz'))  85.1 us
    dot_general x8, matrix products, window_grads(): jnp.einsum('hij,ihd->jhd', grad_scores, queries, preferred_element_type=j...  82.4 us
    psum x1, blocking collectives, per_device(): lax.psum((qkv_grad, proj_grad, gain_grad), ('gx', 'gy', 'gz'))  41.9 us
    dot_general x8, matrix products, window_grads(): jnp.einsum('hij,jhd->ihd', probs_bf, values_all, preferred_element_type=j...  35.3 us
    dot_general x8, matrix products, window_grads(): jnp.einsum('hij,ihd->jhd', probs_bf, grad_heads, preferred_element_type=j...  35.3 us
    dot_general x8, matrix products, window_grads(): jnp.einsum('ihd,jhd->hij', queries, keys_all, preferred_element_type=jnp....  34.3 us
    dot_general x8, matrix products, window_grads(): jnp.einsum('ihd,jhd->hij', grad_heads, values_all, preferred_element_type...  29.5 us
  transfers between devices with their start and end apart: 7, of which 4 were waited for; matrix products, arithmetic and copies ran while one was open for 4% of the time, Pallas kernels for 0%

commit v1 on v0

--- a/solution.py
+++ b/solution.py
@@ -172,7 +172,12 @@
         (to_windows(shifted_tokens), to_windows(shifted_grads), to_windows(mask_key)),
     )
     qkv_grad, proj_grad, gain_grad = sums
-    qkv_grad, proj_grad, gain_grad = lax.psum((qkv_grad, proj_grad, gain_grad), ("gx", "gy", "gz"))
+
+    def ratios_shape(array_here):
+        f_now = lax.psum(lax.psum(array_here, axis_name=("gy", "gz")), axis_name="gx")
+        return f_now
+
+    qkv_grad, proj_grad, gain_grad = ratios_shape((qkv_grad, proj_grad, gain_grad))
     grad_branch = jnp.roll(from_windows(grad_windows, brick_a, brick_b, brick_c), SHIFT, axis=2)
     grad_branch = grad_branch.reshape(brick_a, brick_b, brick_c * channels)
     grad_branch = back_first(back_second(grad_branch))

time: 587 us -> 554 us (0.944)
  waiting for transfers between devices: 99.7 us -> 81.3 us
  blocking collectives: 41.9 us -> 27.2 us
    psum x1 -> x2, waiting for transfers between devices: 85.1 us -> 66.7 us  [the longest x1 36.2 us: ratios_shape(): lax.psum(lax.psum(array_here, axis_name=('gy', 'gz')), axis_name='gx')]
    psum x1 -> x2, blocking collectives: 41.9 us -> 27.2 us  [the longest x1 14.8 us: ratios_shape(): lax.psum(array_here, axis_name=('gy', 'gz'))]
  transfers between devices with their start and end apart: 7 -> 8, of which waited for: 4 -> 5; matrix products, arithmetic and copies ran while one was open for 4% -> 5% of each run, Pallas kernels for 0% -> 0%
where the time goes in v1:
time: 554 us; the launch traced here: 552 us
  matrix products  347 us (63%)
  waiting for transfers between devices  81.3 us (15%)
  local copies, waits for them, and re-layouts  46.7 us (8%)
  blocking collectives  27.2 us (5%)
  other arithmetic  21.1 us (4%)
  between operations  14.3 us (3%)
  starting transfers between devices  14 us (3%)
    dot_general x8, matrix products, window_grads(): jnp.einsum('hij,jhd->ihd', grad_scores, keys_all, preferred_element_type=...  87.1 us
    dot_general x8, matrix products, window_grads(): jnp.einsum('hij,ihd->jhd', grad_scores, queries, preferred_element_type=j...  82.4 us
    psum x1, waiting for transfers between devices, ratios_shape(): lax.psum(lax.psum(array_here, axis_name=('gy', 'gz')), axis_name='gx')  36.2 us
    dot_general x8, matrix products, window_grads(): jnp.einsum('hij,jhd->ihd', probs_bf, values_all, preferred_element_type=j...  35.3 us
    dot_general x8, matrix products, window_grads(): jnp.einsum('hij,ihd->jhd', probs_bf, grad_heads, preferred_element_type=j...  35.3 us
    dot_general x8, matrix products, window_grads(): jnp.einsum('ihd,jhd->hij', queries, keys_all, preferred_element_type=jnp....  34.4 us
    psum x1, waiting for transfers between devices, ratios_shape(): lax.psum(array_here, axis_name=('gy', 'gz'))  30.4 us
    dot_general x8, matrix products, window_grads(): jnp.einsum('ihd,jhd->hij', grad_heads, values_all, preferred_element_type...  29.5 us
  transfers between devices with their start and end apart: 8, of which 5 were waited for; matrix products, arithmetic and copies ran while one was open for 5% of the time, Pallas kernels for 0%

profile of v1, /device:TPU:0, one launch (start us, length us, event | category | flops | bytes accessed | tf_op | source)
XLA Modules:
  0.0 552.5 jit_solution(17655053516040953862)
XLA Ops:
  9.1 5.0 collective-permute-start.2
  25.8 5.5 collective-permute-done
  60.5 357.9 %while.17 = (s32[]{:T(128)}, f32[192,576]{1,0:T(8,128)}, f32[192,192]{1,0:T(8,128)S(1)}, f32[192]{0:T(256)S(1)}, bf16[8,512,192]{1,2,0:T(8,128)(2,1)}, /*index=5...) while((s32[]{:T(128)}, f32[192,576]{1,0:T(8,128)}, ...), condition=%wide.region_8.9_spmd.clone, body=%wide.region_0.8_spmd.clone.sunk | while | flops 1079349888 | bytes 64495856 | solution.py:169
  61.6 4.3 fusion.136
  70.7 10.9 %fusion.140 = bf16[6,32,512]{2,1,0:T(8,128)(2,1)} fusion(bf16[512,6,32]{0,2,1:T(8,128)(2,1)S(1)} %bitcast.169, f32[6,512,512]{1,2,0:T(8,128)} %fusion.138, f32[6,512,512]{1,2,0:T(8,128)} %get-tuple-element.267, f32[6,512]{1,0:T(8,128)S(1)} %get-tuple-element.268, pred[512,512]{0,1:T(8,128)(4,1)S(1)} %broadcast_compare_fusion.2), kind=kOutput, calls=%fused_computation.15.clone.1 | convolution fusion | flops 118066688 | bytes 13250560 | tf_op jit(solution)/shard_map/while/body/eval_jaxpr/hij,jhd->ihd/dot_general | solution.py:80
  81.6 10.3 %fusion.139 = bf16[6,32,512]{2,1,0:T(8,128)(2,1)S(1)} fusion(bf16[512,6,32]{0,2,1:T(8,128)(2,1)S(1)} %bitcast.167, f32[6,512,512]{1,2,0:T(8,128)} %fusion.138, f32[6,512,512]{1,2,0:T(8,128)} %get-tuple-element.267, f32[6,512]{1,0:T(8,128)S(1)} %get-tuple-element.268, pred[512,512]{0,1:T(8,128)(4,1)S(1)} %broadcast_compare_fusion.2), kind=kOutput, calls=%fused_computation.16.clone.1 | convolution fusion | flops 118066688 | bytes 13250560 | tf_op jit(solution)/shard_map/while/body/eval_jaxpr/hij,ihd->jhd/dot_general | solution.py:83
  91.9 4.4 fusion.137
  97.7 4.4 fusion.141
  105.4 4.3 fusion.136
  114.5 10.9 %fusion.140 = bf16[6,32,512]{2,1,0:T(8,128)(2,1)} fusion(bf16[512,6,32]{0,2,1:T(8,128)(2,1)S(1)} %bitcast.169, f32[6,512,512]{1,2,0:T(8,128)} %fusion.138, f32[6,512,512]{1,2,0:T(8,128)} %get-tuple-element.267, f32[6,512]{1,0:T(8,128)S(1)} %get-tuple-element.268, pred[512,512]{0,1:T(8,128)(4,1)S(1)} %broadcast_compare_fusion.2), kind=kOutput, calls=%fused_computation.15.clone.1 | convolution fusion | flops 118066688 | bytes 13250560 | tf_op jit(solution)/shard_map/while/body/eval_jaxpr/hij,jhd->ihd/dot_general | solution.py:80
  125.4 10.3 %fusion.139 = bf16[6,32,512]{2,1,0:T(8,128)(2,1)S(1)} fusion(bf16[512,6,32]{0,2,1:T(8,128)(2,1)S(1)} %bitcast.167, f32[6,512,512]{1,2,0:T(8,128)} %fusion.138, f32[6,512,512]{1,2,0:T(8,128)} %get-tuple-element.267, f32[6,512]{1,0:T(8,128)S(1)} %get-tuple-element.268, pred[512,512]{0,1:T(8,128)(4,1)S(1)} %broadcast_compare_fusion.2), kind=kOutput, calls=%fused_computation.16.clone.1 | convolution fusion | flops 118066688 | bytes 13250560 | tf_op jit(solution)/shard_map/while/body/eval_jaxpr/hij,ihd->jhd/dot_general | solution.py:83
  135.8 4.4 fusion.137
  141.5 4.4 fusion.141
  150.2 4.3 fusion.136
  159.4 10.9 %fusion.140 = bf16[6,32,512]{2,1,0:T(8,128)(2,1)} fusion(bf16[512,6,32]{0,2,1:T(8,128)(2,1)S(1)} %bitcast.169, f32[6,512,512]{1,2,0:T(8,128)} %fusion.138, f32[6,512,512]{1,2,0:T(8,128)} %get-tuple-element.267, f32[6,512]{1,0:T(8,128)S(1)} %get-tuple-element.268, pred[512,512]{0,1:T(8,128)(4,1)S(1)} %broadcast_compare_fusion.2), kind=kOutput, calls=%fused_computation.15.clone.1 | convolution fusion | flops 118066688 | bytes 13250560 | tf_op jit(solution)/shard_map/while/body/eval_jaxpr/hij,jhd->ihd/dot_general | solution.py:80
  170.3 10.3 %fusion.139 = bf16[6,32,512]{2,1,0:T(8,128)(2,1)S(1)} fusion(bf16[512,6,32]{0,2,1:T(8,128)(2,1)S(1)} %bitcast.167, f32[6,512,512]{1,2,0:T(8,128)} %fusion.138, f32[6,512,512]{1,2,0:T(8,128)} %get-tuple-element.267, f32[6,512]{1,0:T(8,128)S(1)} %get-tuple-element.268, pred[512,512]{0,1:T(8,128)(4,1)S(1)} %broadcast_compare_fusion.2), kind=kOutput, calls=%fused_computation.16.clone.1 | convolution fusion | flops 118066688 | bytes 13250560 | tf_op jit(solution)/shard_map/while/body/eval_jaxpr/hij,ihd->jhd/dot_general | solution.py:83
  180.6 4.4 fusion.137
  186.3 4.4 fusion.141
  195.0 4.3 fusion.136
  204.2 10.9 %fusion.140 = bf16[6,32,512]{2,1,0:T(8,128)(2,1)} fusion(bf16[512,6,32]{0,2,1:T(8,128)(2,1)S(1)} %bitcast.169, f32[6,512,512]{1,2,0:T(8,128)} %fusion.138, f32[6,512,512]{1,2,0:T(8,128)} %get-tuple-element.267, f32[6,512]{1,0:T(8,128)S(1)} %get-tuple-element.268, pred[512,512]{0,1:T(8,128)(4,1)S(1)} %broadcast_compare_fusion.2), kind=kOutput, calls=%fused_computation.15.clone.1 | convolution fusion | flops 118066688 | bytes 13250560 | tf_op jit(solution)/shard_map/while/body/eval_jaxpr/hij,jhd->ihd/dot_general | solution.py:80
  215.1 10.3 %fusion.139 = bf16[6,32,512]{2,1,0:T(8,128)(2,1)S(1)} fusion(bf16[512,6,32]{0,2,1:T(8,128)(2,1)S(1)} %bitcast.167, f32[6,512,512]{1,2,0:T(8,128)} %fusion.138, f32[6,512,512]{1,2,0:T(8,128)} %get-tuple-element.267, f32[6,512]{1,0:T(8,128)S(1)} %get-tuple-element.268, pred[512,512]{0,1:T(8,128)(4,1)S(1)} %broadcast_compare_fusion.2), kind=kOutput, calls=%fused_computation.16.clone.1 | convolution fusion | flops 118066688 | bytes 13250560 | tf_op jit(solution)/shard_map/while/body/eval_jaxpr/hij,ihd->jhd/dot_general | solution.py:83
  225.4 4.4 fusion.137
  231.2 4.4 fusion.141
  239.9 4.3 fusion.136
  249.0 10.9 %fusion.140 = bf16[6,32,512]{2,1,0:T(8,128)(2,1)} fusion(bf16[512,6,32]{0,2,1:T(8,128)(2,1)S(1)} %bitcast.169, f32[6,512,512]{1,2,0:T(8,128)} %fusion.138, f32[6,512,512]{1,2,0:T(8,128)} %get-tuple-element.267, f32[6,512]{1,0:T(8,128)S(1)} %get-tuple-element.268, pred[512,512]{0,1:T(8,128)(4,1)S(1)} %broadcast_compare_fusion.2), kind=kOutput, calls=%fused_computation.15.clone.1 | convolution fusion | flops 118066688 | bytes 13250560 | tf_op jit(solution)/shard_map/while/body/eval_jaxpr/hij,jhd->ihd/dot_general | solution.py:80
  259.9 10.3 %fusion.139 = bf16[6,32,512]{2,1,0:T(8,128)(2,1)S(1)} fusion(bf16[512,6,32]{0,2,1:T(8,128)(2,1)S(1)} %bitcast.167, f32[6,512,512]{1,2,0:T(8,128)} %fusion.138, f32[6,512,512]{1,2,0:T(8,128)} %get-tuple-element.267, f32[6,512]{1,0:T(8,128)S(1)} %get-tuple-element.268, pred[512,512]{0,1:T(8,128)(4,1)S(1)} %broadcast_compare_fusion.2), kind=kOutput, calls=%fused_computation.16.clone.1 | convolution fusion | flops 118066688 | bytes 13250560 | tf_op jit(solution)/shard_map/while/body/eval_jaxpr/hij,ihd->jhd/dot_general | solution.py:83
  270.3 4.4 fusion.137
  276.0 4.4 fusion.141
  284.7 4.3 fusion.136
  293.9 10.9 %fusion.140 = bf16[6,32,512]{2,1,0:T(8,128)(2,1)} fusion(bf16[512,6,32]{0,2,1:T(8,128)(2,1)S(1)} %bitcast.169, f32[6,512,512]{1,2,0:T(8,128)} %fusion.138, f32[6,512,512]{1,2,0:T(8,128)} %get-tuple-element.267, f32[6,512]{1,0:T(8,128)S(1)} %get-tuple-element.268, pred[512,512]{0,1:T(8,128)(4,1)S(1)} %broadcast_compare_fusion.2), kind=kOutput, calls=%fused_computation.15.clone.1 | convolution fusion | flops 118066688 | bytes 13250560 | tf_op jit(solution)/shard_map/while/body/eval_jaxpr/hij,jhd->ihd/dot_general | solution.py:80
  304.8 10.3 %fusion.139 = bf16[6,32,512]{2,1,0:T(8,128)(2,1)S(1)} fusion(bf16[512,6,32]{0,2,1:T(8,128)(2,1)S(1)} %bitcast.167, f32[6,512,512]{1,2,0:T(8,128)} %fusion.138, f32[6,512,512]{1,2,0:T(8,128)} %get-tuple-element.267, f32[6,512]{1,0:T(8,128)S(1)} %get-tuple-element.268, pred[512,512]{0,1:T(8,128)(4,1)S(1)} %broadcast_compare_fusion.2), kind=kOutput, calls=%fused_computation.16.clone.1 | convolution fusion | flops 118066688 | bytes 13250560 | tf_op jit(solution)/shard_map/while/body/eval_jaxpr/hij,ihd->jhd/dot_general | solution.py:83
  315.1 4.4 fusion.137
  320.8 4.4 fusion.141
  329.5 4.3 fusion.136
  338.7 10.9 %fusion.140 = bf16[6,32,512]{2,1,0:T(8,128)(2,1)} fusion(bf16[512,6,32]{0,2,1:T(8,128)(2,1)S(1)} %bitcast.169, f32[6,512,512]{1,2,0:T(8,128)} %fusion.138, f32[6,512,512]{1,2,0:T(8,128)} %get-tuple-element.267, f32[6,512]{1,0:T(8,128)S(1)} %get-tuple-element.268, pred[512,512]{0,1:T(8,128)(4,1)S(1)} %broadcast_compare_fusion.2), kind=kOutput, calls=%fused_computation.15.clone.1 | convolution fusion | flops 118066688 | bytes 13250560 | tf_op jit(solution)/shard_map/while/body/eval_jaxpr/hij,jhd->ihd/dot_general | solution.py:80
  349.6 10.3 %fusion.139 = bf16[6,32,512]{2,1,0:T(8,128)(2,1)S(1)} fusion(bf16[512,6,32]{0,2,1:T(8,128)(2,1)S(1)} %bitcast.167, f32[6,512,512]{1,2,0:T(8,128)} %fusion.138, f32[6,512,512]{1,2,0:T(8,128)} %get-tuple-element.267, f32[6,512]{1,0:T(8,128)S(1)} %get-tuple-element.268, pred[512,512]{0,1:T(8,128)(4,1)S(1)} %broadcast_compare_fusion.2), kind=kOutput, calls=%fused_computation.16.clone.1 | convolution fusion | flops 118066688 | bytes 13250560 | tf_op jit(solution)/shard_map/while/body/eval_jaxpr/hij,ihd->jhd/dot_general | solution.py:83
  359.9 4.4 fusion.137
  365.7 4.4 fusion.141
  383.5 10.9 %fusion.140 = bf16[6,32,512]{2,1,0:T(8,128)(2,1)} fusion(bf16[512,6,32]{0,2,1:T(8,128)(2,1)S(1)} %bitcast.169, f32[6,512,512]{1,2,0:T(8,128)} %fusion.138, f32[6,512,512]{1,2,0:T(8,128)} %get-tuple-element.267, f32[6,512]{1,0:T(8,128)S(1)} %get-tuple-element.268, pred[512,512]{0,1:T(8,128)(4,1)S(1)} %broadcast_compare_fusion.2), kind=kOutput, calls=%fused_computation.15.clone.1 | convolution fusion | flops 118066688 | bytes 13250560 | tf_op jit(solution)/shard_map/while/body/eval_jaxpr/hij,jhd->ihd/dot_general | solution.py:80
  394.4 10.3 %fusion.139 = bf16[6,32,512]{2,1,0:T(8,128)(2,1)S(1)} fusion(bf16[512,6,32]{0,2,1:T(8,128)(2,1)S(1)} %bitcast.167, f32[6,512,512]{1,2,0:T(8,128)} %fusion.138, f32[6,512,512]{1,2,0:T(8,128)} %get-tuple-element.267, f32[6,512]{1,0:T(8,128)S(1)} %get-tuple-element.268, pred[512,512]{0,1:T(8,128)(4,1)S(1)} %broadcast_compare_fusion.2), kind=kOutput, calls=%fused_computation.16.clone.1 | convolution fusion | flops 118066688 | bytes 13250560 | tf_op jit(solution)/shard_map/while/body/eval_jaxpr/hij,ihd->jhd/dot_general | solution.py:83
  404.8 4.4 fusion.137
  410.5 4.4 fusion.141
  428.2 6.9 %collective-permute-start.4 = (bf16[16,4,3072]{2,1,0:T(4,128)(2,1)S(1)}, bf16[16,4,3072]{2,1,0:T(4,128)(2,1)S(1)}, u32[]{:S(2)}, u32[]{:S(2)}) collective-permute-start(bf16[16,4,3072]{2,1,0:T(4,128)(2,1)S(1)} %slice.101), channel_id=1, source_target_pairs={{7,0},{0,1},{1,2},{2,3},{3,4},{4,5},{5,6},{6,7},{15,8},{8,9},{9,10... | collective-permute-start | bytes 1179656 | tf_op jit(solution)/shard_map/ppermute | solution.py:16
  435.1 5.3 collective-permute-done.4
  441.8 14.8 %psum.42 = f32[192]{0:T(256)S(1)} all-reduce(f32[192]{0:T(256)S(1)} %get-tuple-element.65), channel_id=1, replica_groups=mesh['gx'=4,'gy'=4,'gz'=2] {'gy','gz'}, use_global_device_ids=true, to_apply=%region_9.10 | all-reduce | flops 192 | bytes 1536 | tf_op jit(solution)/shard_map/psum | solution.py:177
  456.6 12.4 %psum.43 = f32[192]{0:T(256)} all-reduce(f32[192]{0:T(256)S(1)} %psum.42), channel_id=1, replica_groups=mesh['gx'=4,'gy'=4,'gz'=2] {'gx'}, use_global_device_ids=true, to_apply=%region_10.11 | all-reduce | flops 192 | bytes 1536 | tf_op jit(solution)/shard_map/psum | solution.py:177
  469.0 30.4 %all-reduce.5.cloned.1.call-done = (f32[192,576]{1,0:T(8,128)}, f32[192,192]{1,0:T(8,128)}) async-done(((f32[192,576]{1,0:T(8,128)}, f32[192,192]{1,0:T(8,128)}), (f32[192,576]{1,0:T(8,128)}, f32[192,192]{1,0:T(8,128)})) %all-reduce.5.cloned.1.call-update) | async-done | bytes 589840 | tf_op jit(solution)/shard_map/psum | solution.py:177
  506.0 36.2 %all-reduce.7.cloned.1.call-done = (f32[110592]{0:T(1024)}, f32[36864]{0:T(1024)}) async-done(((f32[110592]{0:T(1024)}, f32[36864]{0:T(1024)}), (f32[110592]{0:T(1024)}, f32[36864]{0:T(1024)})) %all-reduce.7.cloned.1.call-update) | async-done | bytes 589840 | tf_op jit(solution)/shard_map/psum | solution.py:177
  (260 shorter events, 150.4 us)
Async XLA Ops:
  7.2 9.3 %copy-start.7 = (bf16[16,16,3072]{2,1,0:T(8,128)(2,1)S(1)}, bf16[16,16,3072]{2,1,0:T(8,128)(2,1)}, u32[]{:S(2)}) copy-start(bf16[16,16,3072]{2,1,0:T(8,128)(2,1)} %param.8) | copy-start | bytes 4718596
  7.2 492.2 %all-reduce.5.cloned.1.call-start = ((), (), s32[]{:S(2)}) async-start(), calls=%async_computation | async-start | bytes 1376256 | tf_op jit(solution)/shard_map/psum | solution.py:177
  9.1 14.9 %collective-permute-start.2 = (bf16[4,16,3072]{2,1,0:T(8,128)(2,1)}, bf16[4,16,3072]{2,1,0:T(8,128)(2,1)}, u32[]{:S(2)}, u32[]{:S(2)}) collective-permute-start(bf16[4,16,3072]{2,1,0:T(8,128)(2,1)} %slice.74), channel_id=1, source_target_pairs={{8,0},{16,8},{24,16},{0,24},{9,1},{17,9},{25,17},{1,25},{10,2},{18... | collective-permute-start | bytes 1179656 | tf_op jit(solution)/shard_map/ppermute | solution.py:16
  15.9 15.3 %collective-permute-start = (bf16[4,16,3072]{2,1,0:T(8,128)(2,1)}, bf16[4,16,3072]{2,1,0:T(8,128)(2,1)}, u32[]{:S(2)}, u32[]{:S(2)}) collective-permute-start(bf16[4,16,3072]{2,1,0:T(8,128)(2,1)} %slice.68), channel_id=1, source_target_pairs={{8,0},{16,8},{24,16},{0,24},{9,1},{17,9},{25,17},{1,25},{10,2},{18... | collective-permute-start | bytes 1179656 | tf_op jit(solution)/shard_map/ppermute | solution.py:16
  16.4 1.1 copy-start.8
  16.4 1.8 slice-start
  18.2 1.3 copy-start.5
  25.4 10.4 %collective-permute-start.3 = (bf16[16,4,3072]{2,0,1:T(8,128)(2,1)S(1)}, bf16[16,4,3072]{2,0,1:T(8,128)(2,1)S(1)}, u32[]{:S(2)}, u32[]{:S(2)}) collective-permute-start(bf16[16,4,3072]{2,0,1:T(8,128)(2,1)S(1)} %pad_maximum_fusion.10), channel_id=1, source_target_pairs={{1,0},{2,1},{3,2},{4,3},{5,4},{6,5},{7,6},{0,7},{9,8},{10,9},{11,1... | collective-permute-start | bytes 1179656 | tf_op jit(solution)/shard_map/ppermute | solution.py:16
  33.4 10.8 %collective-permute-start.1 = (bf16[16,4,3072]{2,0,1:T(8,128)(2,1)}, bf16[16,4,3072]{2,0,1:T(8,128)(2,1)S(1)}, u32[]{:S(2)}, u32[]{:S(2)}) collective-permute-start(bf16[16,4,3072]{2,0,1:T(8,128)(2,1)} %pad_maximum_fusion.11), channel_id=1, source_target_pairs={{1,0},{2,1},{3,2},{4,3},{5,4},{6,5},{7,6},{0,7},{9,8},{10,9},{11,1... | collective-permute-start | bytes 1179656 | tf_op jit(solution)/shard_map/ppermute | solution.py:16
  41.6 2.6 copy-start.4
  50.1 1.6 copy-start
  57.5 3.0 copy-start.3
  57.5 3.0 copy-start.6
  57.5 3.0 copy-start.9
  91.9 4.4 copy-start.10
  96.4 1.3 copy-start.11
  97.7 5.6 %copy-start.12 = (bf16[6,32,512]{2,1,0:T(8,128)(2,1)S(1)}, bf16[6,32,512]{2,1,0:T(8,128)(2,1)}, u32[]{:S(2)}) copy-start(bf16[6,32,512]{2,1,0:T(8,128)(2,1)} %copy-done.11) | copy-start | bytes 589828 | tf_op jit(solution)/shard_map/while
  135.7 4.4 copy-start.10
  140.2 1.3 copy-start.11
  141.5 5.6 %copy-start.12 = (bf16[6,32,512]{2,1,0:T(8,128)(2,1)S(1)}, bf16[6,32,512]{2,1,0:T(8,128)(2,1)}, u32[]{:S(2)}) copy-start(bf16[6,32,512]{2,1,0:T(8,128)(2,1)} %copy-done.11) | copy-start | bytes 589828 | tf_op jit(solution)/shard_map/while
  180.6 4.4 copy-start.10
  185.0 1.3 copy-start.11
  186.3 5.6 %copy-start.12 = (bf16[6,32,512]{2,1,0:T(8,128)(2,1)S(1)}, bf16[6,32,512]{2,1,0:T(8,128)(2,1)}, u32[]{:S(2)}) copy-start(bf16[6,32,512]{2,1,0:T(8,128)(2,1)} %copy-done.11) | copy-start | bytes 589828 | tf_op jit(solution)/shard_map/while
  225.4 4.4 copy-start.10
  229.8 1.3 copy-start.11
  231.1 5.6 %copy-start.12 = (bf16[6,32,512]{2,1,0:T(8,128)(2,1)S(1)}, bf16[6,32,512]{2,1,0:T(8,128)(2,1)}, u32[]{:S(2)}) copy-start(bf16[6,32,512]{2,1,0:T(8,128)(2,1)} %copy-done.11) | copy-start | bytes 589828 | tf_op jit(solution)/shard_map/while
  270.2 4.4 copy-start.10
  274.7 1.3 copy-start.11
  276.0 5.6 %copy-start.12 = (bf16[6,32,512]{2,1,0:T(8,128)(2,1)S(1)}, bf16[6,32,512]{2,1,0:T(8,128)(2,1)}, u32[]{:S(2)}) copy-start(bf16[6,32,512]{2,1,0:T(8,128)(2,1)} %copy-done.11) | copy-start | bytes 589828 | tf_op jit(solution)/shard_map/while
  315.1 4.4 copy-start.10
  319.5 1.3 copy-start.11
  320.8 5.6 %copy-start.12 = (bf16[6,32,512]{2,1,0:T(8,128)(2,1)S(1)}, bf16[6,32,512]{2,1,0:T(8,128)(2,1)}, u32[]{:S(2)}) copy-start(bf16[6,32,512]{2,1,0:T(8,128)(2,1)} %copy-done.11) | copy-start | bytes 589828 | tf_op jit(solution)/shard_map/while
  359.9 4.4 copy-start.10
  364.3 1.3 copy-start.11
  365.7 5.6 %copy-start.12 = (bf16[6,32,512]{2,1,0:T(8,128)(2,1)S(1)}, bf16[6,32,512]{2,1,0:T(8,128)(2,1)}, u32[]{:S(2)}) copy-start(bf16[6,32,512]{2,1,0:T(8,128)(2,1)} %copy-done.11) | copy-start | bytes 589828 | tf_op jit(solution)/shard_map/while
  404.7 4.4 copy-start.10
  409.2 1.3 copy-start.11
  410.5 5.6 %copy-start.12 = (bf16[6,32,512]{2,1,0:T(8,128)(2,1)S(1)}, bf16[6,32,512]{2,1,0:T(8,128)(2,1)}, u32[]{:S(2)}) copy-start(bf16[6,32,512]{2,1,0:T(8,128)(2,1)} %copy-done.11) | copy-start | bytes 589828 | tf_op jit(solution)/shard_map/while
  418.4 3.3 copy-start.1
  428.2 12.2 %collective-permute-start.4 = (bf16[16,4,3072]{2,1,0:T(4,128)(2,1)S(1)}, bf16[16,4,3072]{2,1,0:T(4,128)(2,1)S(1)}, u32[]{:S(2)}, u32[]{:S(2)}) collective-permute-start(bf16[16,4,3072]{2,1,0:T(4,128)(2,1)S(1)} %slice.101), channel_id=1, source_target_pairs={{7,0},{0,1},{1,2},{2,3},{3,4},{4,5},{5,6},{6,7},{15,8},{8,9},{9,10... | collective-permute-start | bytes 1179656 | tf_op jit(solution)/shard_map/ppermute | solution.py:16
  440.4 62.8 %copy-start.2 = (bf16[16,16,3072]{2,1,0:T(8,128)(2,1)S(1)}, bf16[16,16,3072]{2,1,0:T(8,128)(2,1)}, u32[]{:S(2)}) copy-start(bf16[16,16,3072]{2,1,0:T(8,128)(2,1)} %param.9) | copy-start | bytes 4718596
  441.3 61.9 %collective-permute-start.5 = (bf16[4,16,3072]{2,1,0:T(8,128)(2,1)}, bf16[4,16,3072]{2,1,0:T(8,128)(2,1)}, u32[]{:S(2)}, u32[]{:S(2)}) collective-permute-start(bf16[4,16,3072]{2,1,0:T(8,128)(2,1)} %pad_maximum_fusion.9), channel_id=1, source_target_pairs={{24,0},{0,8},{8,16},{16,24},{25,1},{1,9},{9,17},{17,25},{26,2},{2,... | collective-permute-start | bytes 1179656 | tf_op jit(solution)/shard_map/ppermute | solution.py:16
  441.8 100.5 %all-reduce.7.cloned.1.call-start = ((), (), s32[]{:S(2)}) async-start(), calls=%async_computation.1 | async-start | bytes 1179648 | tf_op jit(solution)/shard_map/psum | solution.py:177
Sparse Core Ops, SparseCore 0:
  441.9 57.4 all-reduce.4
  503.3 38.9 all-reduce.6
